TPU v7x, 256 devices: a whole 4x4x8 slice. The times are simulated.
256 devices in a mesh: seq: 8 (over z_lo, x), chan: 32 (over y, z_hi, core).
Axes of the slice: x: 4, y: 4, z: 8 (z_hi: 4, z_lo: 2; z = z_hi * 2 + z_lo), core: 2. Of those that a mesh axis runs over, the one named last changes fastest.
Arguments:
- tokens: bfloat16 [8192, 4096], P('seq', 'chan'), may hold values from -6 to 6
- in_weight: bfloat16 [4096, 3, 4096], P(None, None, 'chan'), may hold values from -0.09375 to 0.09375
- short_taps: float32 [3, 3, 4096], P(None, None, 'chan'), may hold values from -3 to 3
- filter_taps: float32 [8192, 4096], P('seq', 'chan'), may hold values from -1 to 1
- skip_gain: float32 [4096], P('chan'), may hold values from -4 to 4
- out_weight: bfloat16 [4096, 4096], P('chan'), may hold values from -0.1875 to 0.1875
Outputs:
- layer_out: bfloat16 [8192, 4096], P('seq', 'chan')
All inputs are finite; a program needn't handle non-finite values.
Results may differ from a plain program's by a relative error of at most 0.007.
Values may be sent and summed in bfloat16 or wider, within the bound.
No kernel may reach another device: no remote copies, remote signals or barrier semaphores. Data moves between devices by JAX's collectives and lax.ppermute only.
A program may use at most 128 MiB of HBM per device.

v0:
```python
import math

import jax
import jax.numpy as jnp
from jax import lax
from jax.sharding import PartitionSpec as P

COLS = 256


highest = lax.Precision.HIGH


def from_behind(shard, axis, by):
    size = lax.axis_size(axis)
    pairs = [(i, i + by) for i in range(size) if 0 <= i + by < size]
    return lax.ppermute(shard, axis, pairs)


def phase_table(row_count, col_count, period):
    row_index = jnp.arange(row_count, dtype=jnp.int32)[:, None]
    col_index = jnp.arange(col_count, dtype=jnp.int32)[None, :]
    angle = (row_index * col_index % period).astype(jnp.float32) * (2.0 * math.pi / period)
    return (jnp.cos(angle), jnp.sin(angle))


def real_transform(signal, cosine, sines, pattern):
    real_part = jnp.einsum(pattern, cosine, signal, precision=highest)
    imag_part = -jnp.einsum(pattern, sines, signal, precision=highest)
    return (real_part, imag_part)


def complex_transform(real_part, imag_part, cosine, sines, direction, pattern):
    cos_real = jnp.einsum(pattern, cosine, real_part, precision=highest)
    cos_imag = jnp.einsum(pattern, cosine, imag_part, precision=highest)
    sin_real = jnp.einsum(pattern, sines, real_part, precision=highest)
    sin_imag = jnp.einsum(pattern, sines, imag_part, precision=highest)
    return (cos_real - direction * sin_imag, cos_imag + direction * sin_real)


def rotate(real_part, imag_part, cosine, sines, direction):
    return (
        real_part * cosine - direction * imag_part * sines,
        imag_part * cosine + direction * real_part * sines,
    )


def spectrum_product(left, right):
    prod_real = left[0] * right[0] - left[1] * right[1]
    prod_imag = left[0] * right[1] + left[1] * right[0]
    return (prod_real, prod_imag)


def real_inverse(real_part, imag_part, cosine, sines, pattern, length):
    return (
        jnp.einsum(pattern, cosine, real_part, precision=highest)
        - jnp.einsum(pattern, sines, imag_part, precision=highest)
    ) / length


def tables(length):
    full_rows = 2 * length // COLS
    half_rows = full_rows // 2
    period = 2 * length
    first = phase_table(full_rows, half_rows, full_rows)
    twist_cos, twist_sin = phase_table(full_rows, COLS, period)
    twist = (twist_cos[:, :, None], twist_sin[:, :, None])
    second = phase_table(COLS, COLS, COLS)
    last = phase_table(half_rows, full_rows, full_rows)
    return first, twist, second, last


def forward_spectrum(whole_seq, first, twist, second):
    length, narrow = whole_seq.shape
    half_rows = 2 * length // COLS // 2
    laid_out = whole_seq.reshape(half_rows, COLS, narrow)
    real_part, imag_part = real_transform(laid_out, first[0], first[1], "kn,nmc->kmc")
    real_part, imag_part = rotate(real_part, imag_part, twist[0], twist[1], -1.0)
    return complex_transform(
        real_part, imag_part, second[0], second[1], -1.0, "kn,anc->akc"
    )


def inverse_spectrum(real_part, imag_part, twist, second, last, length, narrow):
    real_part, imag_part = complex_transform(
        real_part, imag_part, second[0], second[1], 1.0, "kn,anc->akc"
    )
    real_part, imag_part = rotate(real_part, imag_part, twist[0], twist[1], 1.0)
    values = real_inverse(real_part, imag_part, last[0], last[1], "nk,kmc->nmc", 2 * length)
    return values.reshape(length, narrow)


def to_whole_seq(shard):
    return lax.all_to_all(shard, "seq", split_axis=1, concat_axis=0, tiled=True)


def layer(tokens, in_weight, short_taps, filter_taps, skip_gain, out_weight):
    tok_count = tokens.shape[0]
    chan_count = in_weight.shape[2]
    token_blocks = lax.all_gather(tokens, "chan", axis=0, tiled=False)
    seq_count = lax.axis_size("seq")
    part = out_weight.shape[0] // seq_count
    own_rows = lax.dynamic_slice_in_dim(
        out_weight, lax.axis_index("seq") * part, part, axis=0
    )
    out_rows = lax.all_to_all(own_rows, "chan", split_axis=1, concat_axis=0, tiled=True)
    whole_filter = to_whole_seq(filter_taps)
    length, narrow = whole_filter.shape
    first, twist, second, last = tables(length)
    filter_tables = lax.optimization_barrier((first, twist, second))
    filter_spec = forward_spectrum(whole_filter, *filter_tables)
    flat_weight = in_weight.reshape(in_weight.shape[0], 3 * chan_count)
    token_blocks, out_rows = lax.optimization_barrier((token_blocks, out_rows))
    block_count, _, block_width = token_blocks.shape
    projected = jnp.einsum(
        "jtc,jcn->tn",
        token_blocks,
        flat_weight.reshape(block_count, block_width, -1),
        preferred_element_type=jnp.float32,
    )
    projected = projected.astype(jnp.bfloat16).reshape(tok_count, 3, chan_count)
    previous = from_behind(projected[-2:], "seq", 1)
    extended = jnp.concatenate([previous, projected], axis=0).astype(jnp.float32)
    short_mixed = (
        short_taps[0] * extended[2:]
        + short_taps[1] * extended[1:-1]
        + short_taps[2] * extended[:-2]
    )
    gate_out = short_mixed[:, 0]
    signal = short_mixed[:, 1] * short_mixed[:, 2]
    whole_signal = to_whole_seq(signal.astype(jnp.bfloat16)).astype(jnp.float32)
    signal_spec = forward_spectrum(whole_signal, first, twist, second)
    real_part, imag_part = spectrum_product(signal_spec, filter_spec)
    values = inverse_spectrum(real_part, imag_part, twist, second, last, length, narrow)
    out_parts = lax.all_gather(out_rows, "seq", axis=0, tiled=False)
    values, out_parts = lax.optimization_barrier((values, out_parts))
    convolved = lax.all_to_all(
        values.astype(jnp.bfloat16), "seq", split_axis=0, concat_axis=1, tiled=True
    ).astype(jnp.float32)
    out_block = out_parts.reshape(seq_count, block_count, part, -1).transpose(1, 0, 2, 3)
    hidden = (gate_out * (convolved + skip_gain * signal)).astype(jnp.bfloat16)
    hidden_blocks = lax.all_gather(hidden, "chan", axis=0, tiled=False)
    layer_out = jnp.einsum(
        "jtc,jcn->tn",
        hidden_blocks,
        out_block.reshape(block_count, block_width, -1),
        preferred_element_type=jnp.float32,
    )
    return layer_out.astype(jnp.bfloat16)


def solution(mesh):
    in_specs = (
        P("seq", "chan"),
        P(None, None, "chan"),
        P(None, None, "chan"),
        P("seq", "chan"),
        P("chan"),
        P("chan", None),
    )
    out_specs = P("seq", "chan")
    return jax.shard_map(layer, mesh=mesh, in_specs=in_specs, out_specs=out_specs, check_vma=False)
```

profile of v0, /device:TPU:35, one launch (start us, length us, event | category | flops | bytes accessed | tf_op | source)
XLA Modules:
  0.0 261.5 jit_solution(877631211141965370)
XLA Ops:
  6.5 0.7 all-gather.8.cloned.1.call-update
  7.3 2.1 copy.73
  9.3 5.2 %all-to-all-start.2 = ((f32[1024,8,16]{0,2,1:T(8,128)}), f32[1024,8,16]{0,2,1:T(8,128)S(1)}, u32[]{:S(2)}, u32[]{:S(2)}) async-start(f32[1024,8,16]{0,2,1:T(8,128)} %bitcast.17), calls=%async_computation.2 | async-start | bytes 1048576 | tf_op jit(solution)/shard_map/all_to_all | solution.py:94
  14.5 6.8 %copy.86 = bf16[4096,3,128]{2,1,0:T(4,128)(2,1)} copy(bf16[4096,3,128]{2,0,1:T(8,128)(2,1)} %param.7) | data formatting | bytes 6291456 | tf_op jit(solution)/shard_map/reshape;reshape | solution.py:118
  21.3 9.0 %reshape.203 = bf16[32,128,384]{2,1,0:T(8,128)(2,1)} reshape(bf16[4096,3,128]{2,1,0:T(4,128)(2,1)} %copy.86) | data formatting | bytes 6291456 | tf_op jit(solution)/shard_map/reshape;reshape | solution.py:118
  30.4 0.3 fusion.72
  30.6 1.7 fusion.50
  32.6 0.9 broadcast_multiply_fusion
  33.5 0.7 copy_bitcast_fusion.1
  34.2 11.7 %all-to-all-start = ((bf16[16,32,128]{2,0,1:T(8,128)(2,1)}), bf16[16,32,128]{2,0,1:T(8,128)(2,1)}, u32[]{:S(2)}, u32[]{:S(2)}) async-start(bf16[16,32,128]{2,0,1:T(8,128)(2,1)} %copy_bitcast_fusion.1), calls=%async_computation | async-start | bytes 262144 | tf_op jit(solution)/shard_map/all_to_all | solution.py:106
  45.9 0.3 copy.74
  46.4 0.6 convolution_negate_fusion
  47.0 0.8 multiply_add_fusion.1
  47.9 1.0 copy-done.1
  48.9 1.1 fusion.17
  50.0 6.9 %all-to-all-done = bf16[16,32,128]{2,0,1:T(8,128)(2,1)} async-done(((bf16[16,32,128]{2,0,1:T(8,128)(2,1)}), bf16[16,32,128]{2,0,1:T(8,128)(2,1)}, u32[]{:S(2)}, u32[]{:S(2)}) %all-to-all-start) | async-done | bytes 131104 | tf_op jit(solution)/shard_map/all_to_all | solution.py:106
  56.9 33.6 %all-gather.8.cloned.1.call-done = bf16[32768,128]{1,0:T(8,128)(2,1)} async-done(((bf16[1024,128]{1,0:T(8,128)(2,1)}), bf16[32768,128]{1,0:T(8,128)(2,1)}) %all-gather.8.cloned.1.call-update) | async-done | bytes 8388624 | tf_op jit(solution)/shard_map/all_gather | solution.py:100
  90.5 7.9 %bitcast_convert_fusion = bf16[1024,384]{1,0:T(8,128)(2,1)S(1)} fusion(bf16[32,1024,128]{2,1,0:T(8,128)(2,1)} %bitcast.151, bf16[32,128,384]{2,1,0:T(8,128)(2,1)} %reshape.203), kind=kOutput, calls=%fused_computation.5 | convolution fusion | flops 3221618688 | bytes 12320768 | tf_op jit(solution)/shard_map/jtc,jcn->tn/dot_general | solution.py:115
  98.4 0.9 copy-done.7
  99.3 0.6 slice.35
  99.9 3.0 %collective-permute-start = (bf16[2,3,128]{2,1,0:T(4,128)(2,1)}, bf16[2,3,128]{2,1,0:T(4,128)(2,1)S(1)}, u32[]{:S(2)}, u32[]{:S(2)}) collective-permute-start(bf16[2,3,128]{2,1,0:T(4,128)(2,1)} %slice.35), channel_id=1, source_target_pairs={{0,32},{32,64},{64,96},{96,128},{128,160},{160,192},{192,224},{1,3... | collective-permute-start | bytes 4616 | tf_op jit(solution)/shard_map/ppermute | solution.py:17
  102.9 3.0 %fusion.2 = f32[64,16,256]{2,1,0:T(8,128)} fusion(f32[64,16,256]{2,1,0:T(8,128)S(1)} %fusion.17, f32[64,256,16]{1,0,2:T(8,128)S(1)} %get-tuple-element.30, f32[256,256]{1,0:T(8,128)} %get-tuple-element.21), kind=kOutput, calls=%fused_computation.11 | convolution fusion | flops 403177472 | bytes 3407872 | tf_op jit(solution)/shard_map/kn,anc->akc/dot_general | solution.py:36
  106.0 1.4 copy.68
  107.6 0.4 maximum_convert_fusion
  107.9 1.2 fusion
  109.1 0.8 fusion.49
  109.9 5.3 %all-to-all-start.1 = ((bf16[1024,8,16]{0,2,1:T(8,128)(2,1)}), bf16[1024,8,16]{0,2,1:T(8,128)(2,1)S(1)}, u32[]{:S(2)}, u32[]{:S(2)}) async-start(bf16[1024,8,16]{0,2,1:T(8,128)(2,1)} %bitcast.11), calls=%async_computation.1 | async-start | bytes 524288 | tf_op jit(solution)/shard_map/all_to_all | solution.py:94
  115.2 2.4 fusion.21
  117.6 2.1 fusion.4
  119.9 0.6 all-to-all-done.1
  120.8 0.6 fusion.87
  121.4 1.6 multiply_subtract_fusion.2
  123.1 2.1 fusion.27
  125.1 2.0 fusion.23
  127.2 2.0 fusion.5
  129.3 2.3 multiply_subtract_fusion
  131.5 1.5 fusion.8
  133.1 1.8 fusion.12
  134.9 1.6 convolution_add_fusion
  136.4 1.7 add_bitcast_fusion
  138.1 1.0 fusion.15
  139.1 1.0 fusion.6
  140.3 11.8 %all-gather.10.cloned.1.call-done = bf16[4096,128]{1,0:T(8,128)(2,1)} async-done(((bf16[512,128]{1,0:T(8,128)(2,1)}), bf16[4096,128]{1,0:T(8,128)(2,1)}) %all-gather.10.cloned.1.call-update) | async-done | bytes 1048592 | tf_op jit(solution)/shard_map/all_gather | solution.py:135
  152.1 9.9 %all_to_all.61 = bf16[8,1024,16]{1,2,0:T(8,128)(2,1)S(1)} all-to-all(bf16[8,1024,16]{1,2,0:T(8,128)(2,1)S(1)} %bitcast.149), channel_id=1, replica_groups=mesh['seq'=8,'chan'=32] {'seq'}, dimensions={0} | all-to-all | bytes 524288 | tf_op jit(solution)/shard_map/all_to_all | solution.py:137
  162.2 0.8 copy.84
  163.1 1.5 copy.85
  164.6 84.0 %all-gather.6.cloned.1.call-done = bf16[32,1024,128]{2,1,0:T(8,128)(2,1)} async-done(((bf16[1,1024,128]{2,1,0:T(8,128)(2,1)}), bf16[32,1024,128]{2,1,0:T(8,128)(2,1)}) %all-gather.6.cloned.1.call-update) | async-done | bytes 8388624 | tf_op jit(solution)/shard_map/all_gather | solution.py:142
  248.6 6.4 %fusion.7 = bf16[1024,128]{1,0:T(8,128)(2,1)} fusion(bf16[32,1024,128]{2,1,0:T(8,128)(2,1)} %all-gather.6.cloned.1.call-done, bf16[32,128,128]{2,1,0:T(8,128)(2,1)S(1)} %bitcast.146), kind=kOutput, calls=%fused_computation.21 | convolution fusion | flops 1073872896 | bytes 9699328 | tf_op jit(solution)/shard_map/jtc,jcn->tn/dot_general | solution.py:143
  (38 shorter events, 1.7 us)
Async XLA Ops:
  6.5 27.0 %copy-start = (bf16[128,4096]{1,0:T(8,128)(2,1)S(1)}, bf16[128,4096]{1,0:T(8,128)(2,1)}, u32[]{:S(2)}) copy-start(bf16[128,4096]{1,0:T(8,128)(2,1)} %param.11) | copy-start | bytes 3145732
  6.5 84.0 %all-gather.8.cloned.1.call-start = ((), (), s32[]{:S(2)}) async-start(), calls=%async_computation.5 | async-start | bytes 8650752 | tf_op jit(solution)/shard_map/all_gather | solution.py:100
  9.3 24.9 %all-to-all-start.2 = ((f32[1024,8,16]{0,2,1:T(8,128)}), f32[1024,8,16]{0,2,1:T(8,128)S(1)}, u32[]{:S(2)}, u32[]{:S(2)}) async-start(f32[1024,8,16]{0,2,1:T(8,128)} %bitcast.17), calls=%async_computation.2 | async-start | bytes 1048576 | tf_op jit(solution)/shard_map/all_to_all | solution.py:94
  21.3 12.9 %copy-start.8 = (f32[3,3,128]{2,1,0:T(4,128)S(1)}, f32[3,3,128]{2,1,0:T(4,128)}, u32[]{:S(2)}) copy-start(f32[3,3,128]{2,1,0:T(4,128)} %param.8) | copy-start | bytes 13828
  34.2 22.7 %all-to-all-start = ((bf16[16,32,128]{2,0,1:T(8,128)(2,1)}), bf16[16,32,128]{2,0,1:T(8,128)(2,1)}, u32[]{:S(2)}, u32[]{:S(2)}) async-start(bf16[16,32,128]{2,0,1:T(8,128)(2,1)} %copy_bitcast_fusion.1), calls=%async_computation | async-start | bytes 262144 | tf_op jit(solution)/shard_map/all_to_all | solution.py:106
  47.9 1.0 copy-start.1
  47.9 55.0 %copy-start.3 = (f32[64,256,16]{1,0,2:T(8,128)}, f32[64,256,16]{1,0,2:T(8,128)S(1)}, u32[]{:S(2)}) copy-start(f32[64,256,16]{1,0,2:T(8,128)S(1)} %get-tuple-element.30) | copy-start | bytes 3145732
  98.4 0.9 copy-start.7
  99.9 7.5 %collective-permute-start = (bf16[2,3,128]{2,1,0:T(4,128)(2,1)}, bf16[2,3,128]{2,1,0:T(4,128)(2,1)S(1)}, u32[]{:S(2)}, u32[]{:S(2)}) collective-permute-start(bf16[2,3,128]{2,1,0:T(4,128)(2,1)} %slice.35), channel_id=1, source_target_pairs={{0,32},{32,64},{64,96},{96,128},{128,160},{160,192},{192,224},{1,3... | collective-permute-start | bytes 4616 | tf_op jit(solution)/shard_map/ppermute | solution.py:17
  109.9 7.7 %copy-start.6 = (f32[256,256]{1,0:T(8,128)S(1)}, f32[256,256]{1,0:T(8,128)}, u32[]{:S(2)}) copy-start(f32[256,256]{1,0:T(8,128)} %get-tuple-element.21) | copy-start | bytes 786436
  109.9 10.6 %all-to-all-start.1 = ((bf16[1024,8,16]{0,2,1:T(8,128)(2,1)}), bf16[1024,8,16]{0,2,1:T(8,128)(2,1)S(1)}, u32[]{:S(2)}, u32[]{:S(2)}) async-start(bf16[1024,8,16]{0,2,1:T(8,128)(2,1)} %bitcast.11), calls=%async_computation.1 | async-start | bytes 524288 | tf_op jit(solution)/shard_map/all_to_all | solution.py:94
  115.2 36.9 %all-gather.10.cloned.1.call-start = ((), (), s32[]{:S(2)}) async-start(), calls=%async_computation.6 | async-start | bytes 1179648 | tf_op jit(solution)/shard_map/all_gather | solution.py:135
  115.2 2.4 copy-start.2
  119.7 128.8 %all-gather.6.cloned.1.call-start = ((), (), s32[]{:S(2)}) async-start(), calls=%async_computation.4 | async-start | bytes 8650752 | tf_op jit(solution)/shard_map/all_gather | solution.py:142
  127.2 2.1 copy-start.4
  127.2 2.1 copy-start.5
  139.1 22.9 %copy-start.9 = (f32[128]{0:T(128)S(1)}, f32[128]{0:T(128)}, u32[]{:S(2)}) copy-start(f32[128]{0:T(128)} %param.10) | copy-start | bytes 1540
Sparse Core Ops, SparseCore 0:
  9.9 80.6 all-gather.7
  119.8 32.2 all-gather.9
  163.2 85.3 all-gather.5
where the time goes:
time: 262 us; the launch traced here: 261 us
  waiting for transfers between devices  138 us (53%)
  matrix products  43.5 us (17%)
  local copies, waits for them, and re-layouts  25.9 us (10%)
  starting transfers between devices  25.4 us (10%)
  between operations  13.4 us (5%)
  blocking collectives  9.86 us (4%)
  other arithmetic  5.76 us (2%)
    all_gather x1, waiting for transfers between devices, layer(): hidden_blocks = lax.all_gather(hidden, 'chan', axis=0, tiled=False)  84 us
    all_gather x1, waiting for transfers between devices, layer(): token_blocks = lax.all_gather(tokens, 'chan', axis=0, tiled=False)  33.6 us
    another operation x2, local copies, waits for them, and re-layouts, layer(): flat_weight.reshape(block_count, block_width, -1)  15.8 us
    all_gather x1, waiting for transfers between devices, layer(): out_parts = lax.all_gather(out_rows, 'seq', axis=0, tiled=False)  11.8 us
    all_to_all x1, starting transfers between devices, layer(): lax.all_to_all(own_rows, 'chan', split_axis=1, concat_axis=0, tiled=True)  11.7 us
    all_to_all x2, starting transfers between devices, to_whole_seq(): return lax.all_to_all(shard, 'seq', split_axis=1, concat_axis=0, tiled=True)  10.5 us
    all_to_all x1, blocking collectives, layer(): lax.all_to_all(values.astype(jnp.bfloat16), 'seq', split_axis=0, concat_a...  9.86 us
    dot_general x1, matrix products, layer(): jnp.einsum('jtc,jcn->tn', token_blocks, flat_weight.reshape(block_count,...  7.85 us
  transfers between devices with their start and end apart: 7, of which 5 were waited for; matrix products, arithmetic and copies ran while one was open for 21% of the time, Pallas kernels for 0%

commit v1 on v0

--- a/solution.py
+++ b/solution.py
@@ -132,8 +132,9 @@
     signal_spec = forward_spectrum(whole_signal, first, twist, second)
     real_part, imag_part = spectrum_product(signal_spec, filter_spec)
     values = inverse_spectrum(real_part, imag_part, twist, second, last, length, narrow)
-    out_parts = lax.all_gather(out_rows, "seq", axis=0, tiled=False)
-    values, out_parts = lax.optimization_barrier((values, out_parts))
+    seq_tiled = jnp.broadcast_to(out_rows[None], (seq_count,) + out_rows.shape)
+    values, seq_tiled = lax.optimization_barrier((values, seq_tiled))
+    out_parts = lax.all_to_all(seq_tiled, "seq", split_axis=0, concat_axis=0, tiled=True)
     convolved = lax.all_to_all(
         values.astype(jnp.bfloat16), "seq", split_axis=0, concat_axis=1, tiled=True
     ).astype(jnp.float32)

time: 262 us -> 245 us (0.935)
  waiting for transfers between devices: 138 us -> 104 us
  blocking collectives: 9.86 us -> 25.4 us
    all_gather x1, waiting for transfers between devices: 84 us -> 61.6 us  [layer(): hidden_blocks = lax.all_gather(hidden, 'chan', axis=0, tiled=False)]
    all_to_all x0 -> x1, blocking collectives: none -> 16.6 us  [layer(): lax.all_to_all(seq_tiled, 'seq', split_axis=0, concat_axis=0, tiled=True)]
    all_gather x1 -> x0, waiting for transfers between devices: 11.8 us -> none  [layer(): out_parts = lax.all_gather(out_rows, 'seq', axis=0, tiled=False)]
  transfers between devices with their start and end apart: 7 -> 6, of which waited for: 5 -> 4; matrix products, arithmetic and copies ran while one was open for 21% -> 14% of each run, Pallas kernels for 0% -> 0%
where the time goes in v1:
time: 245 us; the launch traced here: 244 us
  waiting for transfers between devices  104 us (42%)
  matrix products  43.5 us (18%)
  local copies, waits for them, and re-layouts  26.8 us (11%)
  blocking collectives  25.4 us (10%)
  starting transfers between devices  24.9 us (10%)
  between operations  13.7 us (6%)
  other arithmetic  5.73 us (2%)
    all_gather x1, waiting for transfers between devices, layer(): hidden_blocks = lax.all_gather(hidden, 'chan', axis=0, tiled=False)  61.6 us
    all_gather x1, waiting for transfers between devices, layer(): token_blocks = lax.all_gather(tokens, 'chan', axis=0, tiled=False)  33.9 us
    all_to_all x1, blocking collectives, layer(): lax.all_to_all(seq_tiled, 'seq', split_axis=0, concat_axis=0, tiled=True)  16.6 us
    another operation x2, local copies, waits for them, and re-layouts, layer(): flat_weight.reshape(block_count, block_width, -1)  15.8 us
    all_to_all x1, starting transfers between devices, layer(): lax.all_to_all(own_rows, 'chan', split_axis=1, concat_axis=0, tiled=True)  11.7 us
    all_to_all x2, starting transfers between devices, to_whole_seq(): return lax.all_to_all(shard, 'seq', split_axis=1, concat_axis=0, tiled=True)  10.5 us
    all_to_all x1, blocking collectives, layer(): lax.all_to_all(values.astype(jnp.bfloat16), 'seq', split_axis=0, concat_a...  8.75 us
    dot_general x1, matrix products, layer(): jnp.einsum('jtc,jcn->tn', token_blocks, flat_weight.reshape(block_count,...  7.85 us
  transfers between devices with their start and end apart: 6, of which 4 were waited for; matrix products, arithmetic and copies ran while one was open for 14% of the time, Pallas kernels for 0%

profile of v1, /device:TPU:35, one launch (start us, length us, event | category | flops | bytes accessed | tf_op | source)
XLA Modules:
  0.0 244.0 jit_solution(10762433404187475843)
XLA Ops:
  6.5 0.7 all-gather.6.cloned.1.call-update
  7.3 2.0 copy.74
  9.3 5.2 %all-to-all-start.2 = ((f32[1024,8,16]{0,2,1:T(8,128)}), f32[1024,8,16]{0,2,1:T(8,128)S(1)}, u32[]{:S(2)}, u32[]{:S(2)}) async-start(f32[1024,8,16]{0,2,1:T(8,128)} %bitcast.17), calls=%async_computation.2 | async-start | bytes 1048576 | tf_op jit(solution)/shard_map/all_to_all | solution.py:94
  14.5 6.8 %copy.87 = bf16[4096,3,128]{2,1,0:T(4,128)(2,1)} copy(bf16[4096,3,128]{2,0,1:T(8,128)(2,1)} %param.7) | data formatting | bytes 6291456 | tf_op jit(solution)/shard_map/reshape;reshape | solution.py:118
  21.2 9.0 %reshape.203 = bf16[32,128,384]{2,1,0:T(8,128)(2,1)} reshape(bf16[4096,3,128]{2,1,0:T(4,128)(2,1)} %copy.87) | data formatting | bytes 6291456 | tf_op jit(solution)/shard_map/reshape;reshape | solution.py:118
  30.6 1.7 fusion.50
  32.6 0.9 broadcast_multiply_fusion
  33.5 0.7 copy_bitcast_fusion.1
  34.2 11.7 %all-to-all-start = ((bf16[16,32,128]{2,0,1:T(8,128)(2,1)}), bf16[16,32,128]{2,0,1:T(8,128)(2,1)}, u32[]{:S(2)}, u32[]{:S(2)}) async-start(bf16[16,32,128]{2,0,1:T(8,128)(2,1)} %copy_bitcast_fusion.1), calls=%async_computation | async-start | bytes 262144 | tf_op jit(solution)/shard_map/all_to_all | solution.py:106
  45.9 0.3 copy.75
  46.4 0.6 convolution_negate_fusion
  47.0 0.8 multiply_add_fusion.1
  47.8 1.0 copy-done.1
  48.9 1.1 fusion.17
  50.0 6.9 %all-to-all-done = bf16[16,32,128]{2,0,1:T(8,128)(2,1)} async-done(((bf16[16,32,128]{2,0,1:T(8,128)(2,1)}), bf16[16,32,128]{2,0,1:T(8,128)(2,1)}, u32[]{:S(2)}, u32[]{:S(2)}) %all-to-all-start) | async-done | bytes 131104 | tf_op jit(solution)/shard_map/all_to_all | solution.py:106
  56.9 33.9 %all-gather.6.cloned.1.call-done = bf16[32768,128]{1,0:T(8,128)(2,1)} async-done(((bf16[1024,128]{1,0:T(8,128)(2,1)}), bf16[32768,128]{1,0:T(8,128)(2,1)}) %all-gather.6.cloned.1.call-update) | async-done | bytes 8388624 | tf_op jit(solution)/shard_map/all_gather | solution.py:100
  90.8 7.9 %bitcast_convert_fusion = bf16[1024,384]{1,0:T(8,128)(2,1)S(1)} fusion(bf16[32,1024,128]{2,1,0:T(8,128)(2,1)} %bitcast.150, bf16[32,128,384]{2,1,0:T(8,128)(2,1)} %reshape.203), kind=kOutput, calls=%fused_computation.5 | convolution fusion | flops 3221618688 | bytes 12320768 | tf_op jit(solution)/shard_map/jtc,jcn->tn/dot_general | solution.py:115
  98.7 0.9 copy-done.7
  99.6 0.6 slice.35
  100.2 2.7 %collective-permute-start = (bf16[2,3,128]{2,1,0:T(4,128)(2,1)}, bf16[2,3,128]{2,1,0:T(4,128)(2,1)S(1)}, u32[]{:S(2)}, u32[]{:S(2)}) collective-permute-start(bf16[2,3,128]{2,1,0:T(4,128)(2,1)} %slice.35), channel_id=1, source_target_pairs={{0,32},{32,64},{64,96},{96,128},{128,160},{160,192},{192,224},{1,3... | collective-permute-start | bytes 4616 | tf_op jit(solution)/shard_map/ppermute | solution.py:17
  102.9 3.0 %fusion.2 = f32[64,16,256]{2,1,0:T(8,128)} fusion(f32[64,16,256]{2,1,0:T(8,128)S(1)} %fusion.17, f32[64,256,16]{1,0,2:T(8,128)S(1)} %get-tuple-element.30, f32[256,256]{1,0:T(8,128)} %get-tuple-element.21), kind=kOutput, calls=%fused_computation.11 | convolution fusion | flops 403177472 | bytes 3407872 | tf_op jit(solution)/shard_map/kn,anc->akc/dot_general | solution.py:36
  105.9 1.4 copy.69
  107.5 0.4 maximum_convert_fusion
  107.9 1.2 fusion
  109.1 0.8 fusion.49
  109.9 5.3 %all-to-all-start.1 = ((bf16[1024,8,16]{0,2,1:T(8,128)(2,1)}), bf16[1024,8,16]{0,2,1:T(8,128)(2,1)S(1)}, u32[]{:S(2)}, u32[]{:S(2)}) async-start(bf16[1024,8,16]{0,2,1:T(8,128)(2,1)} %bitcast.11), calls=%async_computation.1 | async-start | bytes 524288 | tf_op jit(solution)/shard_map/all_to_all | solution.py:94
  115.2 2.4 fusion.21
  117.7 2.1 fusion.4
  119.7 0.8 all-to-all-done.1
  120.9 0.6 fusion.87
  121.4 1.6 multiply_subtract_fusion.2
  123.1 2.1 fusion.27
  125.2 2.0 fusion.23
  127.2 2.0 fusion.5
  129.3 2.5 %multiply_subtract_fusion = (f32[64,16,256]{2,1,0:T(8,128)S(1)}, f32[64,16,256]{2,1,0:T(8,128)S(1)}) fusion(f32[64,16,256]{2,1,0:T(8,128)S(1)} %copy-done.4, f32[64,16,256]{2,1,0:T(8,128)S(1)} %fusion.5, f32[64,16,256]{2,1,0:T(8,128)S(1)} %copy-done.5, f32[64,16,256]{2,1,0:T(8,128)S(1)} %fusion.23, f32[64,256,16]{1,0,2:T(8,128)S(1)} %get-tuple-element.31), kind=kOutput, calls=%fused_computation.34 | convolution fusion | flops 405667840 | bytes 7340032 | tf_op jit(solution)/shard_map/kn,anc->akc/dot_general | solution.py:36
  131.8 1.5 fusion.8
  133.4 1.5 fusion.12
  134.9 1.6 convolution_add_fusion
  136.5 1.7 add_bitcast_fusion
  138.2 1.0 fusion.15
  139.2 1.0 fusion.6
  140.4 2.1 broadcast_in_dim.2
  142.5 8.7 %all_to_all.66 = bf16[8,1024,16]{1,2,0:T(8,128)(2,1)S(1)} all-to-all(bf16[8,1024,16]{1,2,0:T(8,128)(2,1)S(1)} %bitcast.148), channel_id=1, replica_groups=mesh['seq'=8,'chan'=32] {'seq'}, dimensions={0} | all-to-all | bytes 524288 | tf_op jit(solution)/shard_map/all_to_all | solution.py:138
  151.4 0.8 copy.85
  152.3 16.6 %all_to_all.67 = bf16[8,512,128]{2,1,0:T(8,128)(2,1)S(1)} all-to-all(bf16[8,512,128]{2,1,0:T(8,128)(2,1)} %broadcast_in_dim.2), channel_id=1, replica_groups=mesh['seq'=8,'chan'=32] {'seq'}, dimensions={0} | all-to-all | bytes 2097152 | tf_op jit(solution)/shard_map/all_to_all | solution.py:137
  168.9 0.3 copy.86
  169.2 61.6 %all-gather.4.cloned.1.call-done = bf16[32,1024,128]{2,1,0:T(8,128)(2,1)} async-done(((bf16[1,1024,128]{2,1,0:T(8,128)(2,1)}), bf16[32,1024,128]{2,1,0:T(8,128)(2,1)}) %all-gather.4.cloned.1.call-update) | async-done | bytes 8388624 | tf_op jit(solution)/shard_map/all_gather | solution.py:143
  230.7 6.4 %fusion.7 = bf16[1024,128]{1,0:T(8,128)(2,1)} fusion(bf16[32,1024,128]{2,1,0:T(8,128)(2,1)} %all-gather.4.cloned.1.call-done, bf16[32,128,128]{2,1,0:T(8,128)(2,1)S(1)} %bitcast.145), kind=kOutput, calls=%fused_computation.21 | convolution fusion | flops 1073872896 | bytes 9699328 | tf_op jit(solution)/shard_map/jtc,jcn->tn/dot_general | solution.py:144
  (37 shorter events, 1.7 us)
Async XLA Ops:
  6.5 27.0 %copy-start = (bf16[128,4096]{1,0:T(8,128)(2,1)S(1)}, bf16[128,4096]{1,0:T(8,128)(2,1)}, u32[]{:S(2)}) copy-start(bf16[128,4096]{1,0:T(8,128)(2,1)} %param.11) | copy-start | bytes 3145732
  6.5 84.3 %all-gather.6.cloned.1.call-start = ((), (), s32[]{:S(2)}) async-start(), calls=%async_computation.6 | async-start | bytes 8650752 | tf_op jit(solution)/shard_map/all_gather | solution.py:100
  9.3 24.9 %all-to-all-start.2 = ((f32[1024,8,16]{0,2,1:T(8,128)}), f32[1024,8,16]{0,2,1:T(8,128)S(1)}, u32[]{:S(2)}, u32[]{:S(2)}) async-start(f32[1024,8,16]{0,2,1:T(8,128)} %bitcast.17), calls=%async_computation.2 | async-start | bytes 1048576 | tf_op jit(solution)/shard_map/all_to_all | solution.py:94
  21.2 12.9 %copy-start.8 = (f32[3,3,128]{2,1,0:T(4,128)S(1)}, f32[3,3,128]{2,1,0:T(4,128)}, u32[]{:S(2)}) copy-start(f32[3,3,128]{2,1,0:T(4,128)} %param.8) | copy-start | bytes 13828
  34.2 22.7 %all-to-all-start = ((bf16[16,32,128]{2,0,1:T(8,128)(2,1)}), bf16[16,32,128]{2,0,1:T(8,128)(2,1)}, u32[]{:S(2)}, u32[]{:S(2)}) async-start(bf16[16,32,128]{2,0,1:T(8,128)(2,1)} %copy_bitcast_fusion.1), calls=%async_computation | async-start | bytes 262144 | tf_op jit(solution)/shard_map/all_to_all | solution.py:106
  47.8 1.0 copy-start.1
  47.8 55.1 %copy-start.3 = (f32[64,256,16]{1,0,2:T(8,128)}, f32[64,256,16]{1,0,2:T(8,128)S(1)}, u32[]{:S(2)}) copy-start(f32[64,256,16]{1,0,2:T(8,128)S(1)} %get-tuple-element.30) | copy-start | bytes 3145732
  98.7 0.9 copy-start.7
  100.2 7.2 %collective-permute-start = (bf16[2,3,128]{2,1,0:T(4,128)(2,1)}, bf16[2,3,128]{2,1,0:T(4,128)(2,1)S(1)}, u32[]{:S(2)}, u32[]{:S(2)}) collective-permute-start(bf16[2,3,128]{2,1,0:T(4,128)(2,1)} %slice.35), channel_id=1, source_target_pairs={{0,32},{32,64},{64,96},{96,128},{128,160},{160,192},{192,224},{1,3... | collective-permute-start | bytes 4616 | tf_op jit(solution)/shard_map/ppermute | solution.py:17
  109.9 7.8 %copy-start.6 = (f32[256,256]{1,0:T(8,128)S(1)}, f32[256,256]{1,0:T(8,128)}, u32[]{:S(2)}) copy-start(f32[256,256]{1,0:T(8,128)} %get-tuple-element.21) | copy-start | bytes 786436
  109.9 10.7 %all-to-all-start.1 = ((bf16[1024,8,16]{0,2,1:T(8,128)(2,1)}), bf16[1024,8,16]{0,2,1:T(8,128)(2,1)S(1)}, u32[]{:S(2)}, u32[]{:S(2)}) async-start(bf16[1024,8,16]{0,2,1:T(8,128)(2,1)} %bitcast.11), calls=%async_computation.1 | async-start | bytes 524288 | tf_op jit(solution)/shard_map/all_to_all | solution.py:94
  115.2 115.5 %all-gather.4.cloned.1.call-start = ((), (), s32[]{:S(2)}) async-start(), calls=%async_computation.5 | async-start | bytes 8650752 | tf_op jit(solution)/shard_map/all_gather | solution.py:143
  115.2 2.4 copy-start.2
  127.2 2.1 copy-start.4
  127.2 2.1 copy-start.5
  140.2 11.1 %copy-start.9 = (f32[128]{0:T(128)S(1)}, f32[128]{0:T(128)}, u32[]{:S(2)}) copy-start(f32[128]{0:T(128)} %param.10) | copy-start | bytes 1540
Sparse Core Ops, SparseCore 0:
  9.9 80.8 all-gather.5
  152.4 78.3 all-gather.3

commit v2 on v1

--- a/solution.py
+++ b/solution.py
@@ -25,8 +25,8 @@
 
 
 def real_transform(signal, cosine, sines, pattern):
-    real_part = jnp.einsum(pattern, cosine, signal, precision=highest)
-    imag_part = -jnp.einsum(pattern, sines, signal, precision=highest)
+    real_part = jnp.einsum(pattern, cosine, signal, precision=lax.Precision.DEFAULT)
+    imag_part = -jnp.einsum(pattern, sines, signal, precision=lax.Precision.DEFAULT)
     return (real_part, imag_part)
 
 
@@ -53,8 +53,8 @@
 
 def real_inverse(real_part, imag_part, cosine, sines, pattern, length):
     return (
-        jnp.einsum(pattern, cosine, real_part, precision=highest)
-        - jnp.einsum(pattern, sines, imag_part, precision=highest)
+        jnp.einsum(pattern, cosine, real_part, precision=lax.Precision.DEFAULT)
+        - jnp.einsum(pattern, sines, imag_part, precision=lax.Precision.DEFAULT)
     ) / length
 
 

time: 245 us -> 243 us (level)
  matrix products: 43.5 us -> 41 us
    dot_general x6, matrix products: 5.65 us -> 3.14 us  [the longest x2 1.67 us: real_transform(): jnp.einsum(pattern, sines, signal, precision=lax.Precision.DEFAULT)]
where the time goes in v2:
time: 243 us; the launch traced here: 242 us
  waiting for transfers between devices  106 us (44%)
  matrix products  41 us (17%)
  local copies, waits for them, and re-layouts  26.5 us (11%)
  blocking collectives  25.2 us (10%)
  starting transfers between devices  24.2 us (10%)
  between operations  13.7 us (6%)
  other arithmetic  5.74 us (2%)
    all_gather x1, waiting for transfers between devices, layer(): hidden_blocks = lax.all_gather(hidden, 'chan', axis=0, tiled=False)  61.6 us
    all_gather x1, waiting for transfers between devices, layer(): token_blocks = lax.all_gather(tokens, 'chan', axis=0, tiled=False)  34.8 us
    all_to_all x1, blocking collectives, layer(): lax.all_to_all(seq_tiled, 'seq', split_axis=0, concat_axis=0, tiled=True)  16.5 us
    another operation x2, local copies, waits for them, and re-layouts, layer(): flat_weight.reshape(block_count, block_width, -1)  15.8 us
    all_to_all x1, starting transfers between devices, layer(): lax.all_to_all(own_rows, 'chan', split_axis=1, concat_axis=0, tiled=True)  11.7 us
    all_to_all x2, starting transfers between devices, to_whole_seq(): return lax.all_to_all(shard, 'seq', split_axis=1, concat_axis=0, tiled=True)  10.2 us
    all_to_all x1, blocking collectives, layer(): lax.all_to_all(values.astype(jnp.bfloat16), 'seq', split_axis=0, concat_a...  8.74 us
    dot_general x1, matrix products, layer(): jnp.einsum('jtc,jcn->tn', token_blocks, flat_weight.reshape(block_count,...  7.85 us
  transfers between devices with their start and end apart: 6, of which 4 were waited for; matrix products, arithmetic and copies ran while one was open for 14% of the time, Pallas kernels for 0%

profile of v2, /device:TPU:35, one launch (start us, length us, event | category | flops | bytes accessed | tf_op | source)
XLA Modules:
  0.0 242.0 jit_solution(11537719698915562421)
XLA Ops:
  6.5 0.7 all-gather.6.cloned.1.call-update
  7.3 1.9 copy.74
  9.1 5.2 %all-to-all-start.2 = ((bf16[1024,8,16]{0,2,1:T(8,128)(2,1)}), bf16[1024,8,16]{0,2,1:T(8,128)(2,1)S(1)}, u32[]{:S(2)}, u32[]{:S(2)}) async-start(bf16[1024,8,16]{0,2,1:T(8,128)(2,1)} %bitcast.17), calls=%async_computation.2 | async-start | bytes 524288 | tf_op jit(solution)/shard_map/all_to_all | solution.py:94
  14.6 0.3 fusion.72
  14.9 0.9 broadcast_multiply_fusion
  15.8 0.7 copy_bitcast_fusion.1
  16.4 1.7 fusion.50
  18.2 6.8 %copy.87 = bf16[4096,3,128]{2,1,0:T(4,128)(2,1)} copy(bf16[4096,3,128]{2,0,1:T(8,128)(2,1)} %param.7) | data formatting | bytes 6291456 | tf_op jit(solution)/shard_map/reshape;reshape | solution.py:118
  25.0 9.0 %reshape.203 = bf16[32,128,384]{2,1,0:T(8,128)(2,1)} reshape(bf16[4096,3,128]{2,1,0:T(4,128)(2,1)} %copy.87) | data formatting | bytes 6291456 | tf_op jit(solution)/shard_map/reshape;reshape | solution.py:118
  34.1 11.7 %all-to-all-start = ((bf16[16,32,128]{2,0,1:T(8,128)(2,1)}), bf16[16,32,128]{2,0,1:T(8,128)(2,1)}, u32[]{:S(2)}, u32[]{:S(2)}) async-start(bf16[16,32,128]{2,0,1:T(8,128)(2,1)} %copy_bitcast_fusion.1), calls=%async_computation | async-start | bytes 262144 | tf_op jit(solution)/shard_map/all_to_all | solution.py:106
  46.1 0.3 convolution_negate_fusion
  46.4 0.4 multiply_add_fusion.1
  46.8 1.0 copy-done.1
  47.8 1.1 fusion.17
  48.9 7.7 %all-to-all-done = bf16[16,32,128]{2,0,1:T(8,128)(2,1)} async-done(((bf16[16,32,128]{2,0,1:T(8,128)(2,1)}), bf16[16,32,128]{2,0,1:T(8,128)(2,1)}, u32[]{:S(2)}, u32[]{:S(2)}) %all-to-all-start) | async-done | bytes 131104 | tf_op jit(solution)/shard_map/all_to_all | solution.py:106
  56.6 34.8 %all-gather.6.cloned.1.call-done = bf16[32768,128]{1,0:T(8,128)(2,1)} async-done(((bf16[1024,128]{1,0:T(8,128)(2,1)}), bf16[32768,128]{1,0:T(8,128)(2,1)}) %all-gather.6.cloned.1.call-update) | async-done | bytes 8388624 | tf_op jit(solution)/shard_map/all_gather | solution.py:100
  91.4 7.9 %bitcast_convert_fusion = bf16[1024,384]{1,0:T(8,128)(2,1)S(1)} fusion(bf16[32,1024,128]{2,1,0:T(8,128)(2,1)} %bitcast.150, bf16[32,128,384]{2,1,0:T(8,128)(2,1)} %reshape.203), kind=kOutput, calls=%fused_computation.5 | convolution fusion | flops 3221618688 | bytes 12320768 | tf_op jit(solution)/shard_map/jtc,jcn->tn/dot_general | solution.py:115
  99.3 0.9 copy-done.7
  100.1 0.6 slice.35
  100.7 2.3 collective-permute-start
  103.0 3.0 %fusion.2 = f32[64,16,256]{2,1,0:T(8,128)} fusion(f32[64,16,256]{2,1,0:T(8,128)S(1)} %fusion.17, f32[64,256,16]{1,0,2:T(8,128)S(1)} %get-tuple-element.30, f32[256,256]{1,0:T(8,128)} %get-tuple-element.21), kind=kOutput, calls=%fused_computation.11 | convolution fusion | flops 403177472 | bytes 3407872 | tf_op jit(solution)/shard_map/kn,anc->akc/dot_general | solution.py:36
  106.1 1.4 copy.69
  107.7 0.4 maximum_convert_fusion
  108.0 1.2 fusion
  109.2 0.8 fusion.49
  110.0 5.0 %all-to-all-start.1 = ((bf16[1024,8,16]{0,2,1:T(8,128)(2,1)}), bf16[1024,8,16]{0,2,1:T(8,128)(2,1)S(1)}, u32[]{:S(2)}, u32[]{:S(2)}) async-start(bf16[1024,8,16]{0,2,1:T(8,128)(2,1)} %bitcast.11), calls=%async_computation.1 | async-start | bytes 524288 | tf_op jit(solution)/shard_map/all_to_all | solution.py:94
  115.1 2.4 fusion.21
  117.5 2.1 fusion.4
  119.6 0.8 all-to-all-done.1
  120.7 0.4 fusion.87
  121.1 1.3 multiply_subtract_fusion.2
  122.5 2.1 fusion.27
  124.5 2.0 fusion.23
  126.6 2.0 fusion.5
  128.7 2.3 multiply_subtract_fusion
  131.0 1.8 fusion.8
  132.7 1.5 fusion.12
  134.3 1.6 convolution_add_fusion
  135.9 1.7 add_bitcast_fusion
  137.6 0.3 fusion.15
  137.9 0.3 fusion.6
  138.4 2.1 broadcast_in_dim.2
  140.5 8.7 %all_to_all.66 = bf16[8,1024,16]{1,2,0:T(8,128)(2,1)S(1)} all-to-all(bf16[8,1024,16]{1,2,0:T(8,128)(2,1)S(1)} %bitcast.148), channel_id=1, replica_groups=mesh['seq'=8,'chan'=32] {'seq'}, dimensions={0} | all-to-all | bytes 524288 | tf_op jit(solution)/shard_map/all_to_all | solution.py:138
  149.5 0.8 copy.85
  150.3 16.5 %all_to_all.67 = bf16[8,512,128]{2,1,0:T(8,128)(2,1)S(1)} all-to-all(bf16[8,512,128]{2,1,0:T(8,128)(2,1)} %broadcast_in_dim.2), channel_id=1, replica_groups=mesh['seq'=8,'chan'=32] {'seq'}, dimensions={0} | all-to-all | bytes 2097152 | tf_op jit(solution)/shard_map/all_to_all | solution.py:137
  166.9 0.3 copy.86
  167.1 61.6 %all-gather.4.cloned.1.call-done = bf16[32,1024,128]{2,1,0:T(8,128)(2,1)} async-done(((bf16[1,1024,128]{2,1,0:T(8,128)(2,1)}), bf16[32,1024,128]{2,1,0:T(8,128)(2,1)}) %all-gather.4.cloned.1.call-update) | async-done | bytes 8388624 | tf_op jit(solution)/shard_map/all_gather | solution.py:143
  228.8 6.4 %fusion.7 = bf16[1024,128]{1,0:T(8,128)(2,1)} fusion(bf16[32,1024,128]{2,1,0:T(8,128)(2,1)} %all-gather.4.cloned.1.call-done, bf16[32,128,128]{2,1,0:T(8,128)(2,1)S(1)} %bitcast.144), kind=kOutput, calls=%fused_computation.21 | convolution fusion | flops 1073872896 | bytes 9699328 | tf_op jit(solution)/shard_map/jtc,jcn->tn/dot_general | solution.py:144
  (37 shorter events, 1.6 us)
Async XLA Ops:
  6.5 9.2 %copy-start = (bf16[128,4096]{1,0:T(8,128)(2,1)S(1)}, bf16[128,4096]{1,0:T(8,128)(2,1)}, u32[]{:S(2)}) copy-start(bf16[128,4096]{1,0:T(8,128)(2,1)} %param.11) | copy-start | bytes 3145732
  6.5 84.8 %all-gather.6.cloned.1.call-start = ((), (), s32[]{:S(2)}) async-start(), calls=%async_computation.6 | async-start | bytes 8650752 | tf_op jit(solution)/shard_map/all_gather | solution.py:100
  9.1 24.9 %all-to-all-start.2 = ((bf16[1024,8,16]{0,2,1:T(8,128)(2,1)}), bf16[1024,8,16]{0,2,1:T(8,128)(2,1)S(1)}, u32[]{:S(2)}, u32[]{:S(2)}) async-start(bf16[1024,8,16]{0,2,1:T(8,128)(2,1)} %bitcast.17), calls=%async_computation.2 | async-start | bytes 524288 | tf_op jit(solution)/shard_map/all_to_all | solution.py:94
  25.0 9.0 %copy-start.8 = (f32[3,3,128]{2,1,0:T(4,128)S(1)}, f32[3,3,128]{2,1,0:T(4,128)}, u32[]{:S(2)}) copy-start(f32[3,3,128]{2,1,0:T(4,128)} %param.8) | copy-start | bytes 13828
  34.1 22.5 %all-to-all-start = ((bf16[16,32,128]{2,0,1:T(8,128)(2,1)}), bf16[16,32,128]{2,0,1:T(8,128)(2,1)}, u32[]{:S(2)}, u32[]{:S(2)}) async-start(bf16[16,32,128]{2,0,1:T(8,128)(2,1)} %copy_bitcast_fusion.1), calls=%async_computation | async-start | bytes 262144 | tf_op jit(solution)/shard_map/all_to_all | solution.py:106
  46.8 1.0 copy-start.1
  46.8 56.2 %copy-start.3 = (f32[64,256,16]{1,0,2:T(8,128)}, f32[64,256,16]{1,0,2:T(8,128)S(1)}, u32[]{:S(2)}) copy-start(f32[64,256,16]{1,0,2:T(8,128)S(1)} %get-tuple-element.30) | copy-start | bytes 3145732
  99.2 0.9 copy-start.7
  100.7 6.8 %collective-permute-start = (bf16[2,3,128]{2,1,0:T(4,128)(2,1)}, bf16[2,3,128]{2,1,0:T(4,128)(2,1)S(1)}, u32[]{:S(2)}, u32[]{:S(2)}) collective-permute-start(bf16[2,3,128]{2,1,0:T(4,128)(2,1)} %slice.35), channel_id=1, source_target_pairs={{0,32},{32,64},{64,96},{96,128},{128,160},{160,192},{192,224},{1,3... | collective-permute-start | bytes 4616 | tf_op jit(solution)/shard_map/ppermute | solution.py:17
  110.0 7.5 %copy-start.6 = (f32[256,256]{1,0:T(8,128)S(1)}, f32[256,256]{1,0:T(8,128)}, u32[]{:S(2)}) copy-start(f32[256,256]{1,0:T(8,128)} %get-tuple-element.21) | copy-start | bytes 786436
  110.0 10.4 %all-to-all-start.1 = ((bf16[1024,8,16]{0,2,1:T(8,128)(2,1)}), bf16[1024,8,16]{0,2,1:T(8,128)(2,1)S(1)}, u32[]{:S(2)}, u32[]{:S(2)}) async-start(bf16[1024,8,16]{0,2,1:T(8,128)(2,1)} %bitcast.11), calls=%async_computation.1 | async-start | bytes 524288 | tf_op jit(solution)/shard_map/all_to_all | solution.py:94
  115.1 113.7 %all-gather.4.cloned.1.call-start = ((), (), s32[]{:S(2)}) async-start(), calls=%async_computation.5 | async-start | bytes 8650752 | tf_op jit(solution)/shard_map/all_gather | solution.py:143
  115.1 2.4 %copy-start.2 = (f32[64,256,16]{1,0,2:T(8,128)S(1)}, f32[64,256,16]{1,0,2:T(8,128)}, u32[]{:S(2)}) copy-start(f32[64,256,16]{1,0,2:T(8,128)} %copy-done.1) | copy-start | bytes 3145732
  126.6 2.1 copy-start.4
  126.6 2.1 copy-start.5
  138.3 11.1 %copy-start.9 = (f32[128]{0:T(128)S(1)}, f32[128]{0:T(128)}, u32[]{:S(2)}) copy-start(f32[128]{0:T(128)} %param.10) | copy-start | bytes 1540
Sparse Core Ops, SparseCore 0:
  9.9 81.4 all-gather.5
  150.5 78.2 all-gather.3

commit v3 on v2

--- a/solution.py
+++ b/solution.py
@@ -30,11 +30,11 @@
     return (real_part, imag_part)
 
 
-def complex_transform(real_part, imag_part, cosine, sines, direction, pattern):
-    cos_real = jnp.einsum(pattern, cosine, real_part, precision=highest)
-    cos_imag = jnp.einsum(pattern, cosine, imag_part, precision=highest)
-    sin_real = jnp.einsum(pattern, sines, real_part, precision=highest)
-    sin_imag = jnp.einsum(pattern, sines, imag_part, precision=highest)
+def complex_transform(real_part, imag_part, cosine, sines, direction, pattern, precision=highest):
+    cos_real = jnp.einsum(pattern, cosine, real_part, precision=precision)
+    cos_imag = jnp.einsum(pattern, cosine, imag_part, precision=precision)
+    sin_real = jnp.einsum(pattern, sines, real_part, precision=precision)
+    sin_imag = jnp.einsum(pattern, sines, imag_part, precision=precision)
     return (cos_real - direction * sin_imag, cos_imag + direction * sin_real)
 
 
@@ -70,14 +70,14 @@
     return first, twist, second, last
 
 
-def forward_spectrum(whole_seq, first, twist, second):
+def forward_spectrum(whole_seq, first, twist, second, precision=highest):
     length, narrow = whole_seq.shape
     half_rows = 2 * length // COLS // 2
     laid_out = whole_seq.reshape(half_rows, COLS, narrow)
     real_part, imag_part = real_transform(laid_out, first[0], first[1], "kn,nmc->kmc")
     real_part, imag_part = rotate(real_part, imag_part, twist[0], twist[1], -1.0)
     return complex_transform(
-        real_part, imag_part, second[0], second[1], -1.0, "kn,anc->akc"
+        real_part, imag_part, second[0], second[1], -1.0, "kn,anc->akc", precision
     )
 
 
@@ -108,7 +108,7 @@
     length, narrow = whole_filter.shape
     first, twist, second, last = tables(length)
     filter_tables = lax.optimization_barrier((first, twist, second))
-    filter_spec = forward_spectrum(whole_filter, *filter_tables)
+    filter_spec = forward_spectrum(whole_filter, *filter_tables, precision=lax.Precision.DEFAULT)
     flat_weight = in_weight.reshape(in_weight.shape[0], 3 * chan_count)
     token_blocks, out_rows = lax.optimization_barrier((token_blocks, out_rows))
     block_count, _, block_width = token_blocks.shape

time: 243 us -> 242 us (level)
  matrix products: 41 us -> 37.3 us
    dot_general x12, matrix products: 23.6 us -> 19.8 us  [the longest x3 5.26 us: complex_transform(): sin_real = jnp.einsum(pattern, sines, real_part, precision=precision)]
  transfers between devices with their start and end apart: 6 -> 6, of which waited for: 4 -> 4; matrix products, arithmetic and copies ran while one was open for 14% -> 13% of each run, Pallas kernels for 0% -> 0%
where the time goes in v3:
time: 242 us; the launch traced here: 241 us
  waiting for transfers between devices  104 us (43%)
  matrix products  37.3 us (15%)
  blocking collectives  26.9 us (11%)
  local copies, waits for them, and re-layouts  26.5 us (11%)
  starting transfers between devices  25.2 us (10%)
  between operations  13.7 us (6%)
  other arithmetic  7.62 us (3%)
    all_gather x1, waiting for transfers between devices, layer(): hidden_blocks = lax.all_gather(hidden, 'chan', axis=0, tiled=False)  59.3 us
    all_gather x1, waiting for transfers between devices, layer(): token_blocks = lax.all_gather(tokens, 'chan', axis=0, tiled=False)  32.5 us
    all_to_all x1, blocking collectives, layer(): lax.all_to_all(seq_tiled, 'seq', split_axis=0, concat_axis=0, tiled=True)  18.3 us
    another operation x2, local copies, waits for them, and re-layouts, layer(): flat_weight.reshape(block_count, block_width, -1)  15.8 us
    all_to_all x1, starting transfers between devices, layer(): lax.all_to_all(own_rows, 'chan', split_axis=1, concat_axis=0, tiled=True)  11.7 us
    all_to_all x2, starting transfers between devices, to_whole_seq(): return lax.all_to_all(shard, 'seq', split_axis=1, concat_axis=0, tiled=True)  10.8 us
    all_to_all x1, blocking collectives, layer(): lax.all_to_all(values.astype(jnp.bfloat16), 'seq', split_axis=0, concat_a...  8.6 us
    all_to_all x1, waiting for transfers between devices, layer(): lax.all_to_all(own_rows, 'chan', split_axis=1, concat_axis=0, tiled=True)  8.31 us
  transfers between devices with their start and end apart: 6, of which 4 were waited for; matrix products, arithmetic and copies ran while one was open for 13% of the time, Pallas kernels for 0%

profile of v3, /device:TPU:35, one launch (start us, length us, event | category | flops | bytes accessed | tf_op | source)
XLA Modules:
  0.0 240.9 jit_solution(17752910158780730782)
XLA Ops:
  6.5 0.7 all-gather.6.cloned.1.call-update
  7.3 1.9 copy.74
  9.1 5.2 %all-to-all-start.2 = ((bf16[1024,8,16]{0,2,1:T(8,128)(2,1)}), bf16[1024,8,16]{0,2,1:T(8,128)(2,1)S(1)}, u32[]{:S(2)}, u32[]{:S(2)}) async-start(bf16[1024,8,16]{0,2,1:T(8,128)(2,1)} %bitcast.17), calls=%async_computation.2 | async-start | bytes 524288 | tf_op jit(solution)/shard_map/all_to_all | solution.py:94
  14.3 0.9 fusion.74
  15.2 0.9 fusion.72
  16.1 0.9 broadcast_multiply_fusion
  17.0 0.7 copy_bitcast_fusion.1
  17.7 1.7 fusion.50
  19.5 6.8 %copy.87 = bf16[4096,3,128]{2,1,0:T(4,128)(2,1)} copy(bf16[4096,3,128]{2,0,1:T(8,128)(2,1)} %param.7) | data formatting | bytes 6291456 | tf_op jit(solution)/shard_map/reshape;reshape | solution.py:118
  26.3 9.0 %reshape.203 = bf16[32,128,384]{2,1,0:T(8,128)(2,1)} reshape(bf16[4096,3,128]{2,1,0:T(4,128)(2,1)} %copy.87) | data formatting | bytes 6291456 | tf_op jit(solution)/shard_map/reshape;reshape | solution.py:118
  35.3 0.6 slice_bitcast_fusion.3
  35.9 0.6 multiply_bitcast_fusion
  36.5 11.7 %all-to-all-start = ((bf16[16,32,128]{2,0,1:T(8,128)(2,1)}), bf16[16,32,128]{2,0,1:T(8,128)(2,1)}, u32[]{:S(2)}, u32[]{:S(2)}) async-start(bf16[16,32,128]{2,0,1:T(8,128)(2,1)} %copy_bitcast_fusion.1), calls=%async_computation | async-start | bytes 262144 | tf_op jit(solution)/shard_map/all_to_all | solution.py:106
  48.8 1.3 multiply_add_fusion.1
  50.2 0.4 fusion.17
  50.6 8.3 %all-to-all-done = bf16[16,32,128]{2,0,1:T(8,128)(2,1)} async-done(((bf16[16,32,128]{2,0,1:T(8,128)(2,1)}), bf16[16,32,128]{2,0,1:T(8,128)(2,1)}, u32[]{:S(2)}, u32[]{:S(2)}) %all-to-all-start) | async-done | bytes 131104 | tf_op jit(solution)/shard_map/all_to_all | solution.py:106
  58.9 32.5 %all-gather.6.cloned.1.call-done = bf16[32768,128]{1,0:T(8,128)(2,1)} async-done(((bf16[1024,128]{1,0:T(8,128)(2,1)}), bf16[32768,128]{1,0:T(8,128)(2,1)}) %all-gather.6.cloned.1.call-update) | async-done | bytes 8388624 | tf_op jit(solution)/shard_map/all_gather | solution.py:100
  91.4 7.9 %bitcast_convert_fusion = bf16[1024,384]{1,0:T(8,128)(2,1)S(1)} fusion(bf16[32,1024,128]{2,1,0:T(8,128)(2,1)} %bitcast.150, bf16[32,128,384]{2,1,0:T(8,128)(2,1)} %reshape.203), kind=kOutput, calls=%fused_computation.5 | convolution fusion | flops 3221618688 | bytes 12320768 | tf_op jit(solution)/shard_map/jtc,jcn->tn/dot_general | solution.py:115
  99.3 0.9 copy-done.5
  100.3 2.7 %collective-permute-start = (bf16[2,3,128]{2,1,0:T(4,128)(2,1)S(1)}, bf16[2,3,128]{2,1,0:T(4,128)(2,1)S(1)}, u32[]{:S(2)}, u32[]{:S(2)}) collective-permute-start(bf16[2,3,128]{2,1,0:T(4,128)(2,1)S(1)} %slice.35), channel_id=1, source_target_pairs={{0,32},{32,64},{64,96},{96,128},{128,160},{160,192},{192,224},{1,3... | collective-permute-start | bytes 4616 | tf_op jit(solution)/shard_map/ppermute | solution.py:17
  103.0 1.4 fusion.2
  104.4 1.4 copy.69
  106.0 0.4 maximum_convert_fusion
  106.5 1.2 fusion
  107.7 0.8 fusion.49
  108.4 5.6 %all-to-all-start.1 = ((bf16[1024,8,16]{0,2,1:T(8,128)(2,1)}), bf16[1024,8,16]{0,2,1:T(8,128)(2,1)}, u32[]{:S(2)}, u32[]{:S(2)}) async-start(bf16[1024,8,16]{0,2,1:T(8,128)(2,1)} %bitcast.143), calls=%async_computation.1 | async-start | bytes 524288 | tf_op jit(solution)/shard_map/all_to_all | solution.py:94
  114.1 1.5 fusion.21
  115.5 1.4 fusion.4
  117.0 2.9 %all-to-all-done.1 = bf16[1024,8,16]{0,2,1:T(8,128)(2,1)} async-done(((bf16[1024,8,16]{0,2,1:T(8,128)(2,1)}), bf16[1024,8,16]{0,2,1:T(8,128)(2,1)}, u32[]{:S(2)}, u32[]{:S(2)}) %all-to-all-start.1) | async-done | bytes 262176 | tf_op jit(solution)/shard_map/all_to_all | solution.py:94
  119.9 1.1 copy.71
  121.1 0.4 fusion.87
  121.6 0.5 multiply_subtract_fusion.2
  122.1 2.1 fusion.27
  124.1 2.0 fusion.23
  126.2 2.0 fusion.5
  128.3 2.3 multiply_subtract_fusion
  130.6 1.8 fusion.8
  132.3 1.5 fusion.12
  133.9 1.6 convolution_add_fusion
  135.5 1.7 add_bitcast_fusion
  137.2 0.3 fusion.15
  137.5 0.3 fusion.6
  138.1 2.1 broadcast_in_dim.2
  140.1 8.6 %all_to_all.66 = bf16[8,1024,16]{1,2,0:T(8,128)(2,1)S(1)} all-to-all(bf16[8,1024,16]{1,2,0:T(8,128)(2,1)S(1)} %bitcast.148), channel_id=1, replica_groups=mesh['seq'=8,'chan'=32] {'seq'}, dimensions={0} | all-to-all | bytes 524288 | tf_op jit(solution)/shard_map/all_to_all | solution.py:138
  148.9 0.8 copy.85
  149.8 18.3 %all_to_all.67 = bf16[8,512,128]{2,1,0:T(8,128)(2,1)S(1)} all-to-all(bf16[8,512,128]{2,1,0:T(8,128)(2,1)} %broadcast_in_dim.2), channel_id=1, replica_groups=mesh['seq'=8,'chan'=32] {'seq'}, dimensions={0} | all-to-all | bytes 2097152 | tf_op jit(solution)/shard_map/all_to_all | solution.py:137
  168.4 59.3 %all-gather.4.cloned.1.call-done = bf16[32,1024,128]{2,1,0:T(8,128)(2,1)} async-done(((bf16[1,1024,128]{2,1,0:T(8,128)(2,1)}), bf16[32,1024,128]{2,1,0:T(8,128)(2,1)}) %all-gather.4.cloned.1.call-update) | async-done | bytes 8388624 | tf_op jit(solution)/shard_map/all_gather | solution.py:143
  227.7 6.4 %fusion.7 = bf16[1024,128]{1,0:T(8,128)(2,1)} fusion(bf16[32,1024,128]{2,1,0:T(8,128)(2,1)} %all-gather.4.cloned.1.call-done, bf16[32,128,128]{2,1,0:T(8,128)(2,1)S(1)} %bitcast.145), kind=kOutput, calls=%fused_computation.21 | convolution fusion | flops 1073872896 | bytes 9699328 | tf_op jit(solution)/shard_map/jtc,jcn->tn/dot_general | solution.py:144
  (41 shorter events, 1.9 us)
Async XLA Ops:
  6.5 10.5 %copy-start = (bf16[128,4096]{1,0:T(8,128)(2,1)S(1)}, bf16[128,4096]{1,0:T(8,128)(2,1)}, u32[]{:S(2)}) copy-start(bf16[128,4096]{1,0:T(8,128)(2,1)} %param.11) | copy-start | bytes 3145732
  6.5 84.9 %all-gather.6.cloned.1.call-start = ((), (), s32[]{:S(2)}) async-start(), calls=%async_computation.6 | async-start | bytes 8650752 | tf_op jit(solution)/shard_map/all_gather | solution.py:100
  9.1 27.4 %all-to-all-start.2 = ((bf16[1024,8,16]{0,2,1:T(8,128)(2,1)}), bf16[1024,8,16]{0,2,1:T(8,128)(2,1)S(1)}, u32[]{:S(2)}, u32[]{:S(2)}) async-start(bf16[1024,8,16]{0,2,1:T(8,128)(2,1)} %bitcast.17), calls=%async_computation.2 | async-start | bytes 524288 | tf_op jit(solution)/shard_map/all_to_all | solution.py:94
  26.3 9.0 %copy-start.10 = (f32[3,3,128]{2,1,0:T(4,128)S(1)}, f32[3,3,128]{2,1,0:T(4,128)}, u32[]{:S(2)}) copy-start(f32[3,3,128]{2,1,0:T(4,128)} %param.8) | copy-start | bytes 13828
  36.5 22.4 %all-to-all-start = ((bf16[16,32,128]{2,0,1:T(8,128)(2,1)}), bf16[16,32,128]{2,0,1:T(8,128)(2,1)}, u32[]{:S(2)}, u32[]{:S(2)}) async-start(bf16[16,32,128]{2,0,1:T(8,128)(2,1)} %copy_bitcast_fusion.1), calls=%async_computation | async-start | bytes 262144 | tf_op jit(solution)/shard_map/all_to_all | solution.py:106
  50.2 52.8 %copy-start.1 = (bf16[64,256,16]{1,0,2:T(8,128)(2,1)}, bf16[64,256,16]{1,0,2:T(8,128)(2,1)S(1)}, u32[]{:S(2)}) copy-start(bf16[64,256,16]{1,0,2:T(8,128)(2,1)S(1)} %get-tuple-element.30) | copy-start | bytes 1572868
  91.4 11.5 %copy-start.4 = (bf16[256,256]{1,0:T(8,128)(2,1)S(1)}, bf16[256,256]{1,0:T(8,128)(2,1)}, u32[]{:S(2)}) copy-start(bf16[256,256]{1,0:T(8,128)(2,1)} %get-tuple-element.21) | copy-start | bytes 393220
  99.3 0.9 copy-start.5
  100.3 5.6 %collective-permute-start = (bf16[2,3,128]{2,1,0:T(4,128)(2,1)S(1)}, bf16[2,3,128]{2,1,0:T(4,128)(2,1)S(1)}, u32[]{:S(2)}, u32[]{:S(2)}) collective-permute-start(bf16[2,3,128]{2,1,0:T(4,128)(2,1)S(1)} %slice.35), channel_id=1, source_target_pairs={{0,32},{32,64},{64,96},{96,128},{128,160},{160,192},{192,224},{1,3... | collective-permute-start | bytes 4616 | tf_op jit(solution)/shard_map/ppermute | solution.py:17
  105.8 0.7 copy-start.9
  108.4 11.4 %all-to-all-start.1 = ((bf16[1024,8,16]{0,2,1:T(8,128)(2,1)}), bf16[1024,8,16]{0,2,1:T(8,128)(2,1)}, u32[]{:S(2)}, u32[]{:S(2)}) async-start(bf16[1024,8,16]{0,2,1:T(8,128)(2,1)} %bitcast.143), calls=%async_computation.1 | async-start | bytes 524288 | tf_op jit(solution)/shard_map/all_to_all | solution.py:94
  114.1 113.6 %all-gather.4.cloned.1.call-start = ((), (), s32[]{:S(2)}) async-start(), calls=%async_computation.5 | async-start | bytes 8650752 | tf_op jit(solution)/shard_map/all_gather | solution.py:143
  117.0 4.6 %copy-start.6 = (f32[64,256]{1,0:T(8,128)S(1)}, f32[64,256]{1,0:T(8,128)}, u32[]{:S(2)}) copy-start(f32[64,256]{1,0:T(8,128)} %get-tuple-element.43) | copy-start | bytes 196612
  117.0 4.6 %copy-start.8 = (f32[64,256]{1,0:T(8,128)S(1)}, f32[64,256]{1,0:T(8,128)}, u32[]{:S(2)}) copy-start(f32[64,256]{1,0:T(8,128)} %get-tuple-element.42) | copy-start | bytes 196612
  126.2 2.1 copy-start.2
  126.2 2.1 copy-start.3
  133.9 1.6 copy-start.7
  137.9 10.9 %copy-start.11 = (f32[128]{0:T(128)S(1)}, f32[128]{0:T(128)}, u32[]{:S(2)}) copy-start(f32[128]{0:T(128)} %param.10) | copy-start | bytes 1540
Sparse Core Ops, SparseCore 0:
  9.9 81.5 all-gather.5
  149.9 77.7 all-gather.3

commit v4 on v3

--- a/solution.py
+++ b/solution.py
@@ -83,7 +83,7 @@
 
 def inverse_spectrum(real_part, imag_part, twist, second, last, length, narrow):
     real_part, imag_part = complex_transform(
-        real_part, imag_part, second[0], second[1], 1.0, "kn,anc->akc"
+        real_part, imag_part, second[0], second[1], 1.0, "kn,anc->akc", lax.Precision.DEFAULT
     )
     real_part, imag_part = rotate(real_part, imag_part, twist[0], twist[1], 1.0)
     values = real_inverse(real_part, imag_part, last[0], last[1], "nk,kmc->nmc", 2 * length)
@@ -129,7 +129,9 @@
     gate_out = short_mixed[:, 0]
     signal = short_mixed[:, 1] * short_mixed[:, 2]
     whole_signal = to_whole_seq(signal.astype(jnp.bfloat16)).astype(jnp.float32)
-    signal_spec = forward_spectrum(whole_signal, first, twist, second)
+    signal_spec = forward_spectrum(
+        whole_signal, first, twist, second, precision=lax.Precision.DEFAULT
+    )
     real_part, imag_part = spectrum_product(signal_spec, filter_spec)
     values = inverse_spectrum(real_part, imag_part, twist, second, last, length, narrow)
     seq_tiled = jnp.broadcast_to(out_rows[None], (seq_count,) + out_rows.shape)

time: 242 us -> 238 us (0.983)
  matrix products: 37.3 us -> 33.3 us
  transfers between devices with their start and end apart: 6 -> 6, of which waited for: 4 -> 4; matrix products, arithmetic and copies ran while one was open for 13% -> 14% of each run, Pallas kernels for 0% -> 0%
where the time goes in v4:
time: 238 us; the launch traced here: 237 us
  waiting for transfers between devices  104 us (44%)
  matrix products  33.3 us (14%)
  blocking collectives  26.9 us (11%)
  local copies, waits for them, and re-layouts  26.7 us (11%)
  starting transfers between devices  25.2 us (11%)
  between operations  13.7 us (6%)
  other arithmetic  7.62 us (3%)
    all_gather x1, waiting for transfers between devices, layer(): hidden_blocks = lax.all_gather(hidden, 'chan', axis=0, tiled=False)  59.3 us
    all_gather x1, waiting for transfers between devices, layer(): token_blocks = lax.all_gather(tokens, 'chan', axis=0, tiled=False)  32.5 us
    all_to_all x1, blocking collectives, layer(): lax.all_to_all(seq_tiled, 'seq', split_axis=0, concat_axis=0, tiled=True)  18.2 us
    another operation x2, local copies, waits for them, and re-layouts, layer(): flat_weight.reshape(block_count, block_width, -1)  15.8 us
    all_to_all x1, starting transfers between devices, layer(): lax.all_to_all(own_rows, 'chan', split_axis=1, concat_axis=0, tiled=True)  11.7 us
    all_to_all x2, starting transfers between devices, to_whole_seq(): return lax.all_to_all(shard, 'seq', split_axis=1, concat_axis=0, tiled=True)  10.8 us
    all_to_all x1, blocking collectives, layer(): lax.all_to_all(values.astype(jnp.bfloat16), 'seq', split_axis=0, concat_a...  8.62 us
    all_to_all x1, waiting for transfers between devices, layer(): lax.all_to_all(own_rows, 'chan', split_axis=1, concat_axis=0, tiled=True)  8.31 us
  transfers between devices with their start and end apart: 6, of which 4 were waited for; matrix products, arithmetic and copies ran while one was open for 14% of the time, Pallas kernels for 0%

profile of v4, /device:TPU:35, one launch (start us, length us, event | category | flops | bytes accessed | tf_op | source)
XLA Modules:
  0.0 237.0 jit_solution(2181487047356230155)
XLA Ops:
  6.5 0.7 all-gather.6.cloned.1.call-update
  7.3 1.9 copy.74
  9.1 5.2 %all-to-all-start.2 = ((bf16[1024,8,16]{0,2,1:T(8,128)(2,1)}), bf16[1024,8,16]{0,2,1:T(8,128)(2,1)S(1)}, u32[]{:S(2)}, u32[]{:S(2)}) async-start(bf16[1024,8,16]{0,2,1:T(8,128)(2,1)} %bitcast.17), calls=%async_computation.2 | async-start | bytes 524288 | tf_op jit(solution)/shard_map/all_to_all | solution.py:94
  14.3 0.9 fusion.74
  15.2 0.9 fusion.72
  16.1 0.9 broadcast_multiply_fusion
  17.0 0.7 copy_bitcast_fusion.1
  17.7 1.7 fusion.50
  19.5 6.8 %copy.87 = bf16[4096,3,128]{2,1,0:T(4,128)(2,1)} copy(bf16[4096,3,128]{2,0,1:T(8,128)(2,1)} %param.7) | data formatting | bytes 6291456 | tf_op jit(solution)/shard_map/reshape;reshape | solution.py:118
  26.3 9.0 %reshape.203 = bf16[32,128,384]{2,1,0:T(8,128)(2,1)} reshape(bf16[4096,3,128]{2,1,0:T(4,128)(2,1)} %copy.87) | data formatting | bytes 6291456 | tf_op jit(solution)/shard_map/reshape;reshape | solution.py:118
  35.3 0.6 slice_bitcast_fusion.3
  35.9 0.6 multiply_bitcast_fusion
  36.5 11.7 %all-to-all-start = ((bf16[16,32,128]{2,0,1:T(8,128)(2,1)}), bf16[16,32,128]{2,0,1:T(8,128)(2,1)}, u32[]{:S(2)}, u32[]{:S(2)}) async-start(bf16[16,32,128]{2,0,1:T(8,128)(2,1)} %copy_bitcast_fusion.1), calls=%async_computation | async-start | bytes 262144 | tf_op jit(solution)/shard_map/all_to_all | solution.py:106
  48.8 1.3 multiply_add_fusion.1
  50.2 0.4 fusion.17
  50.6 8.3 %all-to-all-done = bf16[16,32,128]{2,0,1:T(8,128)(2,1)} async-done(((bf16[16,32,128]{2,0,1:T(8,128)(2,1)}), bf16[16,32,128]{2,0,1:T(8,128)(2,1)}, u32[]{:S(2)}, u32[]{:S(2)}) %all-to-all-start) | async-done | bytes 131104 | tf_op jit(solution)/shard_map/all_to_all | solution.py:106
  58.9 32.5 %all-gather.6.cloned.1.call-done = bf16[32768,128]{1,0:T(8,128)(2,1)} async-done(((bf16[1024,128]{1,0:T(8,128)(2,1)}), bf16[32768,128]{1,0:T(8,128)(2,1)}) %all-gather.6.cloned.1.call-update) | async-done | bytes 8388624 | tf_op jit(solution)/shard_map/all_gather | solution.py:100
  91.4 7.9 %bitcast_convert_fusion = bf16[1024,384]{1,0:T(8,128)(2,1)S(1)} fusion(bf16[32,1024,128]{2,1,0:T(8,128)(2,1)} %bitcast.150, bf16[32,128,384]{2,1,0:T(8,128)(2,1)} %reshape.203), kind=kOutput, calls=%fused_computation.5 | convolution fusion | flops 3221618688 | bytes 12320768 | tf_op jit(solution)/shard_map/jtc,jcn->tn/dot_general | solution.py:115
  99.3 0.9 copy-done.5
  100.3 2.7 %collective-permute-start = (bf16[2,3,128]{2,1,0:T(4,128)(2,1)S(1)}, bf16[2,3,128]{2,1,0:T(4,128)(2,1)S(1)}, u32[]{:S(2)}, u32[]{:S(2)}) collective-permute-start(bf16[2,3,128]{2,1,0:T(4,128)(2,1)S(1)} %slice.35), channel_id=1, source_target_pairs={{0,32},{32,64},{64,96},{96,128},{128,160},{160,192},{192,224},{1,3... | collective-permute-start | bytes 4616 | tf_op jit(solution)/shard_map/ppermute | solution.py:17
  103.0 1.4 fusion.2
  104.4 1.4 copy.69
  106.0 0.4 maximum_convert_fusion
  106.5 1.2 fusion
  107.7 0.8 fusion.49
  108.4 5.6 %all-to-all-start.1 = ((bf16[1024,8,16]{0,2,1:T(8,128)(2,1)}), bf16[1024,8,16]{0,2,1:T(8,128)(2,1)}, u32[]{:S(2)}, u32[]{:S(2)}) async-start(bf16[1024,8,16]{0,2,1:T(8,128)(2,1)} %bitcast.143), calls=%async_computation.1 | async-start | bytes 524288 | tf_op jit(solution)/shard_map/all_to_all | solution.py:94
  114.1 1.5 fusion.21
  115.5 1.4 fusion.4
  117.0 2.9 %all-to-all-done.1 = bf16[1024,8,16]{0,2,1:T(8,128)(2,1)} async-done(((bf16[1024,8,16]{0,2,1:T(8,128)(2,1)}), bf16[1024,8,16]{0,2,1:T(8,128)(2,1)}, u32[]{:S(2)}, u32[]{:S(2)}) %all-to-all-start.1) | async-done | bytes 262176 | tf_op jit(solution)/shard_map/all_to_all | solution.py:94
  119.9 1.1 copy.71
  121.1 0.4 fusion.87
  121.6 0.5 multiply_subtract_fusion.2
  122.1 1.4 fusion.27
  123.4 1.4 fusion.23
  124.8 1.4 fusion.5
  126.3 1.6 multiply_subtract_fusion
  128.0 1.2 fusion.8
  129.2 1.2 fusion.12
  130.4 1.2 convolution_add_fusion
  131.7 1.6 add_bitcast_fusion
  133.3 0.3 fusion.15
  133.6 0.3 fusion.6
  134.1 2.1 broadcast_in_dim.2
  136.2 8.6 %all_to_all.66 = bf16[8,1024,16]{1,2,0:T(8,128)(2,1)S(1)} all-to-all(bf16[8,1024,16]{1,2,0:T(8,128)(2,1)S(1)} %bitcast.148), channel_id=1, replica_groups=mesh['seq'=8,'chan'=32] {'seq'}, dimensions={0} | all-to-all | bytes 524288 | tf_op jit(solution)/shard_map/all_to_all | solution.py:140
  145.1 0.8 copy.85
  145.9 18.2 %all_to_all.67 = bf16[8,512,128]{2,1,0:T(8,128)(2,1)S(1)} all-to-all(bf16[8,512,128]{2,1,0:T(8,128)(2,1)} %broadcast_in_dim.2), channel_id=1, replica_groups=mesh['seq'=8,'chan'=32] {'seq'}, dimensions={0} | all-to-all | bytes 2097152 | tf_op jit(solution)/shard_map/all_to_all | solution.py:139
  164.5 59.3 %all-gather.4.cloned.1.call-done = bf16[32,1024,128]{2,1,0:T(8,128)(2,1)} async-done(((bf16[1,1024,128]{2,1,0:T(8,128)(2,1)}), bf16[32,1024,128]{2,1,0:T(8,128)(2,1)}) %all-gather.4.cloned.1.call-update) | async-done | bytes 8388624 | tf_op jit(solution)/shard_map/all_gather | solution.py:145
  223.8 6.4 %fusion.7 = bf16[1024,128]{1,0:T(8,128)(2,1)} fusion(bf16[32,1024,128]{2,1,0:T(8,128)(2,1)} %all-gather.4.cloned.1.call-done, bf16[32,128,128]{2,1,0:T(8,128)(2,1)S(1)} %bitcast.145), kind=kOutput, calls=%fused_computation.21 | convolution fusion | flops 1073872896 | bytes 9699328 | tf_op jit(solution)/shard_map/jtc,jcn->tn/dot_general | solution.py:146
  (41 shorter events, 2.0 us)
Async XLA Ops:
  6.5 10.5 %copy-start = (bf16[128,4096]{1,0:T(8,128)(2,1)S(1)}, bf16[128,4096]{1,0:T(8,128)(2,1)}, u32[]{:S(2)}) copy-start(bf16[128,4096]{1,0:T(8,128)(2,1)} %param.11) | copy-start | bytes 3145732
  6.5 84.9 %all-gather.6.cloned.1.call-start = ((), (), s32[]{:S(2)}) async-start(), calls=%async_computation.6 | async-start | bytes 8650752 | tf_op jit(solution)/shard_map/all_gather | solution.py:100
  9.1 27.4 %all-to-all-start.2 = ((bf16[1024,8,16]{0,2,1:T(8,128)(2,1)}), bf16[1024,8,16]{0,2,1:T(8,128)(2,1)S(1)}, u32[]{:S(2)}, u32[]{:S(2)}) async-start(bf16[1024,8,16]{0,2,1:T(8,128)(2,1)} %bitcast.17), calls=%async_computation.2 | async-start | bytes 524288 | tf_op jit(solution)/shard_map/all_to_all | solution.py:94
  26.3 9.0 %copy-start.10 = (f32[3,3,128]{2,1,0:T(4,128)S(1)}, f32[3,3,128]{2,1,0:T(4,128)}, u32[]{:S(2)}) copy-start(f32[3,3,128]{2,1,0:T(4,128)} %param.8) | copy-start | bytes 13828
  36.5 22.4 %all-to-all-start = ((bf16[16,32,128]{2,0,1:T(8,128)(2,1)}), bf16[16,32,128]{2,0,1:T(8,128)(2,1)}, u32[]{:S(2)}, u32[]{:S(2)}) async-start(bf16[16,32,128]{2,0,1:T(8,128)(2,1)} %copy_bitcast_fusion.1), calls=%async_computation | async-start | bytes 262144 | tf_op jit(solution)/shard_map/all_to_all | solution.py:106
  50.2 52.8 %copy-start.1 = (bf16[64,256,16]{1,0,2:T(8,128)(2,1)}, bf16[64,256,16]{1,0,2:T(8,128)(2,1)S(1)}, u32[]{:S(2)}) copy-start(bf16[64,256,16]{1,0,2:T(8,128)(2,1)S(1)} %get-tuple-element.30) | copy-start | bytes 1572868
  91.4 11.5 %copy-start.4 = (bf16[256,256]{1,0:T(8,128)(2,1)S(1)}, bf16[256,256]{1,0:T(8,128)(2,1)}, u32[]{:S(2)}) copy-start(bf16[256,256]{1,0:T(8,128)(2,1)} %get-tuple-element.21) | copy-start | bytes 393220
  99.3 0.9 copy-start.5
  100.3 5.6 %collective-permute-start = (bf16[2,3,128]{2,1,0:T(4,128)(2,1)S(1)}, bf16[2,3,128]{2,1,0:T(4,128)(2,1)S(1)}, u32[]{:S(2)}, u32[]{:S(2)}) collective-permute-start(bf16[2,3,128]{2,1,0:T(4,128)(2,1)S(1)} %slice.35), channel_id=1, source_target_pairs={{0,32},{32,64},{64,96},{96,128},{128,160},{160,192},{192,224},{1,3... | collective-permute-start | bytes 4616 | tf_op jit(solution)/shard_map/ppermute | solution.py:17
  105.8 0.7 copy-start.9
  108.4 11.4 %all-to-all-start.1 = ((bf16[1024,8,16]{0,2,1:T(8,128)(2,1)}), bf16[1024,8,16]{0,2,1:T(8,128)(2,1)}, u32[]{:S(2)}, u32[]{:S(2)}) async-start(bf16[1024,8,16]{0,2,1:T(8,128)(2,1)} %bitcast.143), calls=%async_computation.1 | async-start | bytes 524288 | tf_op jit(solution)/shard_map/all_to_all | solution.py:94
  114.1 109.7 %all-gather.4.cloned.1.call-start = ((), (), s32[]{:S(2)}) async-start(), calls=%async_computation.5 | async-start | bytes 8650752 | tf_op jit(solution)/shard_map/all_gather | solution.py:145
  117.0 4.6 %copy-start.6 = (f32[64,256]{1,0:T(8,128)S(1)}, f32[64,256]{1,0:T(8,128)}, u32[]{:S(2)}) copy-start(f32[64,256]{1,0:T(8,128)} %get-tuple-element.43) | copy-start | bytes 196612
  117.0 4.6 %copy-start.7 = (f32[64,256]{1,0:T(8,128)S(1)}, f32[64,256]{1,0:T(8,128)}, u32[]{:S(2)}) copy-start(f32[64,256]{1,0:T(8,128)} %get-tuple-element.42) | copy-start | bytes 196612
  124.8 1.4 copy-start.2
  124.8 1.5 copy-start.3
  129.2 2.5 %copy-start.8 = (f32[64,256]{1,0:T(8,128)S(1)}, f32[64,256]{1,0:T(8,128)}, u32[]{:S(2)}) copy-start(f32[64,256]{1,0:T(8,128)} %fusion.74) | copy-start | bytes 196612
  134.0 10.9 %copy-start.11 = (f32[128]{0:T(128)S(1)}, f32[128]{0:T(128)}, u32[]{:S(2)}) copy-start(f32[128]{0:T(128)} %param.10) | copy-start | bytes 1540
Sparse Core Ops, SparseCore 0:
  9.9 81.5 all-gather.5
  146.1 77.6 all-gather.3
